TPU v7x, 128 devices: a whole 4x4x4 slice. The times are simulated.
128 devices in a mesh: role: 2 (over core), slab: 64 (over x, y, z).
Axes of the slice: x: 4, y: 4, z: 4, core: 2. Of those that a mesh axis runs over, the one named last changes fastest.
Arguments:
- velocity: float32 [4, 128, 128, 256], P(None, 'slab', 'role'), may hold values from -18 to 18
- basis: bfloat16 [256, 128, 128, 256], P(None, 'slab', 'role'), may hold values from -1 to 1, as said below
- mean_flow: float32 [128], replicated, may hold values from 0.2 to 2
- shear: float32 [128], replicated, may hold values from -1 to 1
Outputs:
- advanced: float32 [4, 128, 128, 256], P(None, 'slab', 'role')
- coeffs: float32 [256, 8], replicated
- rfactor: float32 [8, 8], replicated
- directions: float32 [8, 128, 128, 256], P(None, 'slab', 'role')
Inputs may be any that keep to these rules, and one draw needn't show every extreme that they name: Every column of the basis has length within a few percent of one, and distinct columns are nearly orthogonal.
All inputs are finite; a program needn't handle non-finite values.
Results may differ from a plain program's by a relative error of at most 0.00035.
The roundings to bfloat16 on the way count: a program that leaves them out, or rounds other values in their place, can miss the bound.
Values sent between devices are 32-bit elements; how exact they have to be, the bound alone decides.
No kernel may reach another device: no remote copies, remote signals or barrier semaphores. Data moves between devices by JAX's collectives and lax.ppermute only.
A program may use at most 128 MiB of HBM per device.

v0:
```python
import jax
import jax.numpy as jnp
from jax import lax
from jax.sharding import PartitionSpec as P

viscosity = 0.1
time_step = 0.4


def extended(cells, sides, width, closed):
    for axis, dim in sides:
        count = lax.axis_size(axis)
        ends = count if closed else count - 1
        head = lax.slice_in_dim(cells, 0, width, axis=dim)
        tail = lax.slice_in_dim(cells, cells.shape[dim] - width, cells.shape[dim], axis=dim)
        cells = jnp.concatenate(
            [
                lax.ppermute(tail, axis, [(i, (i + 1) % count) for i in range(ends)]),
                cells,
                lax.ppermute(head, axis, [((i + 1) % count, i) for i in range(ends)]),
            ],
            axis=dim,
        )
    return cells


def offset_slice(padded, offset, dimension, length):
    return lax.slice_in_dim(padded, 2 + offset, 2 + offset + length, axis=dimension)


def second_diff(padded, center, dimension, length):
    return (
        -offset_slice(padded, 2, dimension, length)
        + 16.0 * offset_slice(padded, 1, dimension, length)
        - 30.0 * center
        + 16.0 * offset_slice(padded, -1, dimension, length)
        - offset_slice(padded, -2, dimension, length)
    ) / 12.0


def stencil(center, xpadded, ypadded, flow_rows, shear_rows):
    nx_loc = center.shape[1]
    ny_loc = center.shape[2]
    nz_loc = center.shape[3]
    zpadded = jnp.concatenate([center[..., -2:], center, center[..., :2]], axis=3)
    first_x = (
        -offset_slice(xpadded, 2, 1, nx_loc)
        + 8.0 * offset_slice(xpadded, 1, 1, nx_loc)
        - 8.0 * offset_slice(xpadded, -1, 1, nx_loc)
        + offset_slice(xpadded, -2, 1, nx_loc)
    ) / 12.0
    laplace = (
        second_diff(xpadded, center, 1, nx_loc)
        + second_diff(ypadded, center, 2, ny_loc)
        + second_diff(zpadded, center, 3, nz_loc)
    )
    profile = flow_rows[None, None, :, None]
    result = -profile * first_x + viscosity * laplace
    shear_term = shear_rows[None, None, :, None] * center[1:2]
    return jnp.concatenate([result[:1] - shear_term, result[1:]], axis=0)


def segmented_tendency(center, flow_rows, shear_rows):
    xpadded = extended(center, (("slab", 1),), 2, True)
    ypadded = extended(center, (("role", 2),), 2, False)
    return stencil(center, xpadded, ypadded, flow_rows, shear_rows)


def on_device(velocity, basis, mean_flow, shear):
    ny_loc = velocity.shape[2]
    role_index = lax.axis_index("role")
    flow_rows = lax.dynamic_slice_in_dim(mean_flow, role_index * ny_loc, ny_loc)
    shear_rows = lax.dynamic_slice_in_dim(shear, role_index * ny_loc, ny_loc)
    tend_zero = segmented_tendency(velocity, flow_rows, shear_rows)
    segment_one = velocity + time_step * (8.0 / 15.0) * tend_zero
    tend_one = segmented_tendency(segment_one, flow_rows, shear_rows)
    advanced = segment_one + time_step * (5.0 / 12.0 * tend_one - 17.0 / 60.0 * tend_zero)
    snapshots = jnp.concatenate([segment_one, advanced], axis=0)
    flat_snaps = snapshots.reshape(snapshots.shape[0], -1)
    snaps_bf = flat_snaps.astype(jnp.bfloat16)
    basis_rows = basis.reshape(basis.shape[0], -1)
    partial_proj = jnp.einsum("km,sm->ks", basis_rows, snaps_bf, preferred_element_type=jnp.float32)
    coeffs = lax.psum(partial_proj, ("role", "slab"))
    coeffs_bf = coeffs.astype(jnp.bfloat16)
    residual = flat_snaps - jnp.einsum(
        "ks,km->sm", coeffs_bf, basis_rows, preferred_element_type=jnp.float32
    )
    local_gram = jnp.dot(residual, residual.T, precision=lax.Precision.HIGHEST)
    total_gram = lax.psum(local_gram, ("role", "slab"))
    lower_factor = jnp.linalg.cholesky(total_gram)
    directions = jax.scipy.linalg.solve_triangular(lower_factor, residual, lower=True)
    return (advanced, coeffs, lower_factor.T, directions.reshape(snapshots.shape))


def solution(mesh):
    return jax.shard_map(
        on_device,
        mesh=mesh,
        in_specs=(P(None, "slab", "role", None), P(None, "slab", "role", None), P(), P()),
        out_specs=(P(None, "slab", "role", None), P(), P(), P(None, "slab", "role", None)),
        check_vma=False,
    )
```

profile of v0, /device:TPU:1, one launch (start us, length us, event | category | flops | bytes accessed | tf_op | source)
XLA Modules:
  0.0 226.0 jit_solution(16287235402208856212)
XLA Ops:
  0.6 1.4 copy.23
  2.0 2.5 %collective-permute-start.1 = (f32[4,2,64,256]{3,0,2,1:T(4,128)S(1)}, f32[4,2,64,256]{3,0,2,1:T(4,128)S(1)}, u32[]{:S(2)}, u32[]{:S(2)}) collective-permute-start(f32[4,2,64,256]{3,0,2,1:T(4,128)S(1)} %copy.23), channel_id=1, source_target_pairs={{0,1},{1,2},{2,3},{3,4},{4,5},{5,6},{6,7},{7,8},{8,9},{9,10},{10,1... | collective-permute-start | bytes 1572872 | tf_op jit(solution)/shard_map/ppermute | solution.py:18
  4.6 6.8 %collective-permute-start = (f32[4,2,64,256]{3,0,2,1:T(4,128)S(1)}, f32[4,2,64,256]{3,0,2,1:T(4,128)S(1)}, u32[]{:S(2)}, u32[]{:S(2)}) collective-permute-start(f32[4,2,64,256]{3,0,2,1:T(4,128)S(1)} %copy.23), channel_id=1, source_target_pairs={{1,0},{2,1},{3,2},{4,3},{5,4},{6,5},{7,6},{8,7},{9,8},{10,9},{11,1... | collective-permute-start | bytes 1572872 | tf_op jit(solution)/shard_map/ppermute | solution.py:20
  11.4 2.8 %collective-permute-start.2 = (f32[4,2,2,256]{3,0,2,1:T(4,128)S(1)}, f32[4,2,2,256]{3,0,2,1:T(4,128)S(1)}, u32[]{:S(2)}, u32[]{:S(2)}) collective-permute-start(f32[4,2,2,256]{3,0,2,1:T(4,128)S(1)} %get-tuple-element.12), channel_id=1, source_target_pairs={{64,0},{65,1},{66,2},{67,3},{68,4},{69,5},{70,6},{71,7},{72,8},{73... | collective-permute-start | bytes 49160 | tf_op jit(solution)/shard_map/ppermute | solution.py:20
  14.3 1.3 collective-permute-start.3
  16.5 1.0 slice_multiply_fusion.3
  18.2 1.5 constant_dynamic-update-slice_fusion.1
  19.7 3.2 %collective-permute-done.1 = f32[4,2,64,256]{3,0,2,1:T(4,128)S(1)} collective-permute-done((f32[4,2,64,256]{3,0,2,1:T(4,128)S(1)}, f32[4,2,64,256]{3,0,2,1:T(4,128)S(1)}, u32[]{:S(2)}, u32[]{:S(2)}) %collective-permute-start.1) | collective-permute-done | bytes 524320 | tf_op jit(solution)/shard_map/ppermute | solution.py:18
  23.0 1.9 fusion.31
  25.3 1.6 multiply_add_fusion
  27.0 6.9 %collective-permute-start.4 = (f32[4,2,64,256]{3,0,2,1:T(4,128)S(1)}, f32[4,2,64,256]{3,0,2,1:T(4,128)S(1)}, u32[]{:S(2)}, u32[]{:S(2)}) collective-permute-start(f32[4,2,64,256]{3,0,2,1:T(4,128)S(1)} %multiply_add_fusion), channel_id=1, source_target_pairs={{1,0},{2,1},{3,2},{4,3},{5,4},{6,5},{7,6},{8,7},{9,8},{10,9},{11,1... | collective-permute-start | bytes 1572872 | tf_op jit(solution)/shard_map/ppermute | solution.py:20
  33.9 17.9 %copy.34 = bf16[32,8,128,256]{3,1,2,0:T(8,128)(2,1)} copy(bf16[32,8,128,256]{3,2,1,0:T(8,128)(2,1)} %bitcast.33) | data formatting | bytes 33554432
  51.7 3.7 %collective-permute-start.6 = (f32[4,2,2,256]{3,0,2,1:T(4,128)S(1)}, f32[4,2,2,256]{3,0,2,1:T(4,128)S(1)}, u32[]{:S(2)}, u32[]{:S(2)}) collective-permute-start(f32[4,2,2,256]{3,0,2,1:T(4,128)S(1)} %get-tuple-element.10), channel_id=1, source_target_pairs={{64,0},{65,1},{66,2},{67,3},{68,4},{69,5},{70,6},{71,7},{72,8},{73... | collective-permute-start | bytes 49160 | tf_op jit(solution)/shard_map/ppermute | solution.py:20
  55.4 1.5 collective-permute-start.7
  57.1 1.4 collective-permute-done.7
  58.5 2.6 %fusion.12 = f32[4,2,64,256]{3,0,2,1:T(4,128)S(1)} fusion(f32[4,2,2,256]{3,0,2,1:T(4,128)S(1)} %collective-permute-done.7, f32[4,2,64,256]{3,0,2,1:T(4,128)S(1)} %multiply_add_fusion, f32[4,2,2,256]{3,0,2,1:T(4,128)S(1)} %collective-permute-done.6, f32[4,2,64,2]{3,0,2,1:T(4,128)S(1)} %get-tuple-element.9, f32[4,2,64,2]{3,0,2,1:T(4,128)S(1)} %get-tuple-element.8, ...), kind=kLoop, calls=%fused_computation.24 | loop fusion | flops 5505024 | bytes 2138368 | tf_op jit(solution)/shard_map/add | solution.py:58
  61.5 0.9 fusion.47
  62.4 20.8 %fusion.2 = f32[256,8]{0,1:T(8,128)S(1)} fusion(bf16[256,2,64,256]{3,2,1,0:T(8,128)(2,1)} %param.5, f32[4,2,64,256]{3,0,2,1:T(4,128)S(1)} %fusion.47, f32[4,2,64,256]{3,0,2,1:T(4,128)S(1)} %multiply_add_fusion), kind=kOutput, calls=%fused_computation.3 | convolution fusion | flops 135266304 | bytes 17833984 | tf_op jit(solution)/shard_map/km,sm->ks/dot_general | solution.py:82
  84.3 61.8 %psum.14 = f32[256,8]{0,1:T(8,128)S(1)} all-reduce(f32[256,8]{0,1:T(8,128)S(1)} %fusion.2), channel_id=1, replica_groups=mesh['role'=2,'slab'=64] {'role','slab'}, use_global_device_ids=true, to_apply=%region_0.0 | all-reduce | flops 2048 | bytes 16384 | tf_op jit(solution)/shard_map/psum | solution.py:83
  146.1 8.0 %convolution_subtract_fusion = f32[8,32768]{1,0:T(8,128)S(1)} fusion(f32[8,32768]{1,0:T(8,128)S(1)} %bitcast.36, bf16[256,32768]{1,0:T(8,128)(2,1)} %bitcast.34, f32[256,8]{0,1:T(8,128)S(1)} %psum.14), kind=kOutput, calls=%fused_computation | convolution fusion | flops 134481920 | bytes 18882560 | tf_op jit(solution)/shard_map/ks,km->sm/dot_general | solution.py:85
  154.1 2.3 %fusion.59 = f32[8,8]{0,1:T(8,128)S(1)} fusion(f32[8,32768]{1,0:T(8,128)S(1)} %convolution_subtract_fusion), kind=kOutput, calls=%fused_computation.104 | convolution fusion | flops 25165824 | bytes 1048832 | tf_op jit(solution)/shard_map/dot_general | solution.py:88
  156.4 63.8 %psum.15 = f32[8,8]{0,1:T(8,128)S(1)} all-reduce(f32[8,8]{0,1:T(8,128)S(1)} %fusion.59), channel_id=1, replica_groups=mesh['role'=2,'slab'=64] {'role','slab'}, use_global_device_ids=true, to_apply=%region_1.0 | all-reduce | flops 64 | bytes 512 | tf_op jit(solution)/shard_map/psum | solution.py:89
  223.0 1.0 fusion.50
  224.1 1.3 copy.30
  (33 shorter events, 7.2 us)
Async XLA Ops:
  2.0 20.9 %collective-permute-start.1 = (f32[4,2,64,256]{3,0,2,1:T(4,128)S(1)}, f32[4,2,64,256]{3,0,2,1:T(4,128)S(1)}, u32[]{:S(2)}, u32[]{:S(2)}) collective-permute-start(f32[4,2,64,256]{3,0,2,1:T(4,128)S(1)} %copy.23), channel_id=1, source_target_pairs={{0,1},{1,2},{2,3},{3,4},{4,5},{5,6},{6,7},{7,8},{8,9},{9,10},{10,1... | collective-permute-start | bytes 1572872 | tf_op jit(solution)/shard_map/ppermute | solution.py:18
  4.6 18.4 %collective-permute-start = (f32[4,2,64,256]{3,0,2,1:T(4,128)S(1)}, f32[4,2,64,256]{3,0,2,1:T(4,128)S(1)}, u32[]{:S(2)}, u32[]{:S(2)}) collective-permute-start(f32[4,2,64,256]{3,0,2,1:T(4,128)S(1)} %copy.23), channel_id=1, source_target_pairs={{1,0},{2,1},{3,2},{4,3},{5,4},{6,5},{7,6},{8,7},{9,8},{10,9},{11,1... | collective-permute-start | bytes 1572872 | tf_op jit(solution)/shard_map/ppermute | solution.py:20
  11.4 8.3 %collective-permute-start.2 = (f32[4,2,2,256]{3,0,2,1:T(4,128)S(1)}, f32[4,2,2,256]{3,0,2,1:T(4,128)S(1)}, u32[]{:S(2)}, u32[]{:S(2)}) collective-permute-start(f32[4,2,2,256]{3,0,2,1:T(4,128)S(1)} %get-tuple-element.12), channel_id=1, source_target_pairs={{64,0},{65,1},{66,2},{67,3},{68,4},{69,5},{70,6},{71,7},{72,8},{73... | collective-permute-start | bytes 49160 | tf_op jit(solution)/shard_map/ppermute | solution.py:20
  14.3 4.0 %collective-permute-start.3 = (f32[4,2,2,256]{3,0,2,1:T(4,128)S(1)}, f32[4,2,2,256]{3,0,2,1:T(4,128)S(1)}, u32[]{:S(2)}, u32[]{:S(2)}) collective-permute-start(f32[4,2,2,256]{3,0,2,1:T(4,128)S(1)} %get-tuple-element.13), channel_id=1, source_target_pairs={{0,64},{1,65},{2,66},{3,67},{4,68},{5,69},{6,70},{7,71},{8,72},{9,... | collective-permute-start | bytes 49160 | tf_op jit(solution)/shard_map/ppermute | solution.py:18
  26.9 31.6 %collective-permute-start.5 = (f32[4,2,64,256]{3,0,2,1:T(4,128)S(1)}, f32[4,2,64,256]{3,0,2,1:T(4,128)S(1)}, u32[]{:S(2)}, u32[]{:S(2)}) collective-permute-start(f32[4,2,64,256]{3,0,2,1:T(4,128)S(1)} %multiply_add_fusion), channel_id=1, source_target_pairs={{0,1},{1,2},{2,3},{3,4},{4,5},{5,6},{6,7},{7,8},{8,9},{9,10},{10,1... | collective-permute-start | bytes 1572872 | tf_op jit(solution)/shard_map/ppermute | solution.py:18
  27.0 31.5 %collective-permute-start.4 = (f32[4,2,64,256]{3,0,2,1:T(4,128)S(1)}, f32[4,2,64,256]{3,0,2,1:T(4,128)S(1)}, u32[]{:S(2)}, u32[]{:S(2)}) collective-permute-start(f32[4,2,64,256]{3,0,2,1:T(4,128)S(1)} %multiply_add_fusion), channel_id=1, source_target_pairs={{1,0},{2,1},{3,2},{4,3},{5,4},{6,5},{7,6},{8,7},{9,8},{10,9},{11,1... | collective-permute-start | bytes 1572872 | tf_op jit(solution)/shard_map/ppermute | solution.py:20
  33.8 27.6 %copy-start = (f32[4,2,64,256]{3,2,1,0:T(8,128)S(1)}, f32[4,2,64,256]{3,2,1,0:T(8,128)}, u32[]{:S(2)}) copy-start(f32[4,2,64,256]{3,2,1,0:T(8,128)} %param.4) | copy-start | bytes 1572868
  51.7 5.4 %collective-permute-start.6 = (f32[4,2,2,256]{3,0,2,1:T(4,128)S(1)}, f32[4,2,2,256]{3,0,2,1:T(4,128)S(1)}, u32[]{:S(2)}, u32[]{:S(2)}) collective-permute-start(f32[4,2,2,256]{3,0,2,1:T(4,128)S(1)} %get-tuple-element.10), channel_id=1, source_target_pairs={{64,0},{65,1},{66,2},{67,3},{68,4},{69,5},{70,6},{71,7},{72,8},{73... | collective-permute-start | bytes 49160 | tf_op jit(solution)/shard_map/ppermute | solution.py:20
  55.4 3.1 %collective-permute-start.7 = (f32[4,2,2,256]{3,0,2,1:T(4,128)S(1)}, f32[4,2,2,256]{3,0,2,1:T(4,128)S(1)}, u32[]{:S(2)}, u32[]{:S(2)}) collective-permute-start(f32[4,2,2,256]{3,0,2,1:T(4,128)S(1)} %get-tuple-element.11), channel_id=1, source_target_pairs={{0,64},{1,65},{2,66},{3,67},{4,68},{5,69},{6,70},{7,71},{8,72},{9,... | collective-permute-start | bytes 49160 | tf_op jit(solution)/shard_map/ppermute | solution.py:18
  146.1 79.9 %copy-start.1 = (f32[256,8]{0,1:T(8,128)}, f32[256,8]{0,1:T(8,128)S(1)}, u32[]{:S(2)}) copy-start(f32[256,8]{0,1:T(8,128)S(1)} %psum.14) | copy-start | bytes 24580
where the time goes:
time: 227 us; the launch traced here: 226 us
  blocking collectives  126 us (56%)
  matrix products  32.2 us (14%)
  starting transfers between devices  25.6 us (11%)
  local copies, waits for them, and re-layouts  25.1 us (11%)
  other arithmetic  12 us (5%)
  waiting for transfers between devices  4.64 us (2%)
    psum x1, blocking collectives, on_device(): total_gram = lax.psum(local_gram, ('role', 'slab'))  63.8 us
    psum x1, blocking collectives, on_device(): coeffs = lax.psum(partial_proj, ('role', 'slab'))  61.8 us
    unnamed x11, local copies, waits for them, and re-layouts  23.6 us
    dot_general x1, matrix products, on_device(): jnp.einsum('km,sm->ks', basis_rows, snaps_bf, preferred_element_type=jnp....  20.8 us
    ppermute x4, starting transfers between devices, extended(): lax.ppermute(head, axis, [((i + 1) % count, i) for i in range(ends)])  20.3 us
    dot_general x1, matrix products, on_device(): jnp.einsum('ks,km->sm', coeffs_bf, basis_rows, preferred_element_type=jnp...  8.05 us
    ppermute x4, starting transfers between devices, extended(): lax.ppermute(tail, axis, [(i, (i + 1) % count) for i in range(ends)])  5.38 us
    ppermute x4, waiting for transfers between devices, extended(): lax.ppermute(tail, axis, [(i, (i + 1) % count) for i in range(ends)])  4.63 us
  transfers between devices with their start and end apart: 8, of which 2 were waited for; matrix products, arithmetic and copies ran while one was open for 10% of the time, Pallas kernels for 0%

commit v1 on v0

--- a/solution.py
+++ b/solution.py
@@ -80,7 +80,8 @@
     snaps_bf = flat_snaps.astype(jnp.bfloat16)
     basis_rows = basis.reshape(basis.shape[0], -1)
     partial_proj = jnp.einsum("km,sm->ks", basis_rows, snaps_bf, preferred_element_type=jnp.float32)
-    coeffs = lax.psum(partial_proj, ("role", "slab"))
+    pieces = lax.all_gather(partial_proj, ("role", "slab"), axis=0, tiled=False)
+    coeffs = pieces.sum(axis=0)
     coeffs_bf = coeffs.astype(jnp.bfloat16)
     residual = flat_snaps - jnp.einsum(
         "ks,km->sm", coeffs_bf, basis_rows, preferred_element_type=jnp.float32

time: 227 us -> 230 us (1.013)
  blocking collectives: 126 us -> 62.4 us
  waiting for transfers between devices: 4.64 us -> 55.5 us
  between operations: 0.82 us -> 14.2 us
    psum x1 -> x0, blocking collectives: 61.8 us -> none  [on_device(): coeffs = lax.psum(partial_proj, ('role', 'slab'))]
    all_gather x0 -> x1, waiting for transfers between devices: none -> 46.9 us  [on_device(): pieces = lax.all_gather(partial_proj, ('role', 'slab'), axis=0, tiled=False)]
    ppermute x4, waiting for transfers between devices: 4.63 us -> 8.58 us  [extended(): lax.ppermute(tail, axis, [(i, (i + 1) % count) for i in range(ends)])]
  transfers between devices with their start and end apart: 8 -> 9, of which waited for: 2 -> 4; matrix products, arithmetic and copies ran while one was open for 10% -> 10% of each run, Pallas kernels for 0% -> 0%
where the time goes in v1:
time: 230 us; the launch traced here: 229 us
  blocking collectives  62.4 us (27%)
  waiting for transfers between devices  55.5 us (24%)
  matrix products  32.7 us (14%)
  starting transfers between devices  25.7 us (11%)
  local copies, waits for them, and re-layouts  25.3 us (11%)
  between operations  14.2 us (6%)
  other arithmetic  13.4 us (6%)
    psum x1, blocking collectives, on_device(): total_gram = lax.psum(local_gram, ('role', 'slab'))  62.4 us
    all_gather x1, waiting for transfers between devices, on_device(): pieces = lax.all_gather(partial_proj, ('role', 'slab'), axis=0, tiled=False)  46.9 us
    unnamed x11, local copies, waits for them, and re-layouts  23.8 us
    dot_general x1, matrix products, on_device(): jnp.einsum('km,sm->ks', basis_rows, snaps_bf, preferred_element_type=jnp....  21.3 us
    ppermute x4, starting transfers between devices, extended(): lax.ppermute(head, axis, [((i + 1) % count, i) for i in range(ends)])  20.3 us
    ppermute x4, waiting for transfers between devices, extended(): lax.ppermute(tail, axis, [(i, (i + 1) % count) for i in range(ends)])  8.58 us
    dot_general x1, matrix products, on_device(): jnp.einsum('ks,km->sm', coeffs_bf, basis_rows, preferred_element_type=jnp...  8.05 us
    ppermute x4, starting transfers between devices, extended(): lax.ppermute(tail, axis, [(i, (i + 1) % count) for i in range(ends)])  5.38 us
  transfers between devices with their start and end apart: 9, of which 4 were waited for; matrix products, arithmetic and copies ran while one was open for 10% of the time, Pallas kernels for 0%

profile of v1, /device:TPU:1, one launch (start us, length us, event | category | flops | bytes accessed | tf_op | source)
XLA Modules:
  0.0 229.2 jit_solution(15130344477520797424)
XLA Ops:
  7.2 1.4 copy.23
  8.7 2.5 %collective-permute-start.1 = (f32[4,2,64,256]{3,0,2,1:T(4,128)S(1)}, f32[4,2,64,256]{3,0,2,1:T(4,128)S(1)}, u32[]{:S(2)}, u32[]{:S(2)}) collective-permute-start(f32[4,2,64,256]{3,0,2,1:T(4,128)S(1)} %copy.23), channel_id=1, source_target_pairs={{0,1},{1,2},{2,3},{3,4},{4,5},{5,6},{6,7},{7,8},{8,9},{9,10},{10,1... | collective-permute-start | bytes 1572872 | tf_op jit(solution)/shard_map/ppermute | solution.py:18
  11.2 6.8 %collective-permute-start = (f32[4,2,64,256]{3,0,2,1:T(4,128)S(1)}, f32[4,2,64,256]{3,0,2,1:T(4,128)S(1)}, u32[]{:S(2)}, u32[]{:S(2)}) collective-permute-start(f32[4,2,64,256]{3,0,2,1:T(4,128)S(1)} %copy.23), channel_id=1, source_target_pairs={{1,0},{2,1},{3,2},{4,3},{5,4},{6,5},{7,6},{8,7},{9,8},{10,9},{11,1... | collective-permute-start | bytes 1572872 | tf_op jit(solution)/shard_map/ppermute | solution.py:20
  18.0 2.8 %collective-permute-start.2 = (f32[4,2,2,256]{3,0,2,1:T(4,128)S(1)}, f32[4,2,2,256]{3,0,2,1:T(4,128)S(1)}, u32[]{:S(2)}, u32[]{:S(2)}) collective-permute-start(f32[4,2,2,256]{3,0,2,1:T(4,128)S(1)} %get-tuple-element.12), channel_id=1, source_target_pairs={{64,0},{65,1},{66,2},{67,3},{68,4},{69,5},{70,6},{71,7},{72,8},{73... | collective-permute-start | bytes 49160 | tf_op jit(solution)/shard_map/ppermute | solution.py:20
  20.9 1.3 collective-permute-start.3
  24.9 1.5 constant_dynamic-update-slice_fusion.1
  26.4 3.2 %collective-permute-done.1 = f32[4,2,64,256]{3,0,2,1:T(4,128)S(1)} collective-permute-done((f32[4,2,64,256]{3,0,2,1:T(4,128)S(1)}, f32[4,2,64,256]{3,0,2,1:T(4,128)S(1)}, u32[]{:S(2)}, u32[]{:S(2)}) %collective-permute-start.1) | collective-permute-done | bytes 524320 | tf_op jit(solution)/shard_map/ppermute | solution.py:18
  29.6 1.9 fusion.31
  31.9 1.6 multiply_add_fusion
  33.6 6.9 %collective-permute-start.4 = (f32[4,2,64,256]{3,0,2,1:T(4,128)S(1)}, f32[4,2,64,256]{3,0,2,1:T(4,128)S(1)}, u32[]{:S(2)}, u32[]{:S(2)}) collective-permute-start(f32[4,2,64,256]{3,0,2,1:T(4,128)S(1)} %multiply_add_fusion), channel_id=1, source_target_pairs={{1,0},{2,1},{3,2},{4,3},{5,4},{6,5},{7,6},{8,7},{9,8},{10,9},{11,1... | collective-permute-start | bytes 1572872 | tf_op jit(solution)/shard_map/ppermute | solution.py:20
  40.5 3.7 %collective-permute-start.6 = (f32[4,2,2,256]{3,0,2,1:T(4,128)S(1)}, f32[4,2,2,256]{3,0,2,1:T(4,128)S(1)}, u32[]{:S(2)}, u32[]{:S(2)}) collective-permute-start(f32[4,2,2,256]{3,0,2,1:T(4,128)S(1)} %get-tuple-element.10), channel_id=1, source_target_pairs={{64,0},{65,1},{66,2},{67,3},{68,4},{69,5},{70,6},{71,7},{72,8},{73... | collective-permute-start | bytes 49160 | tf_op jit(solution)/shard_map/ppermute | solution.py:20
  44.2 1.5 collective-permute-start.7
  45.9 1.4 collective-permute-done.7
  47.3 4.0 %collective-permute-done.5 = f32[4,2,64,256]{3,0,2,1:T(4,128)S(1)} collective-permute-done((f32[4,2,64,256]{3,0,2,1:T(4,128)S(1)}, f32[4,2,64,256]{3,0,2,1:T(4,128)S(1)}, u32[]{:S(2)}, u32[]{:S(2)}) %collective-permute-start.5) | collective-permute-done | bytes 524320 | tf_op jit(solution)/shard_map/ppermute | solution.py:18
  51.2 2.6 %fusion.12 = f32[4,2,64,256]{3,0,2,1:T(4,128)S(1)} fusion(f32[4,2,2,256]{3,0,2,1:T(4,128)S(1)} %collective-permute-done.7, f32[4,2,64,256]{3,0,2,1:T(4,128)S(1)} %multiply_add_fusion, f32[4,2,2,256]{3,0,2,1:T(4,128)S(1)} %collective-permute-done.6, f32[4,2,64,2]{3,0,2,1:T(4,128)S(1)} %get-tuple-element.9, f32[4,2,64,2]{3,0,2,1:T(4,128)S(1)} %get-tuple-element.8, ...), kind=kLoop, calls=%fused_computation.24 | loop fusion | flops 5505024 | bytes 2138368 | tf_op jit(solution)/shard_map/add | solution.py:58
  55.1 21.3 %fusion.2 = f32[256,8]{0,1:T(8,128)} fusion(bf16[256,2,64,256]{3,2,1,0:T(8,128)(2,1)} %param.5, f32[4,2,64,256]{3,0,2,1:T(4,128)S(1)} %fusion.47, f32[4,2,64,256]{3,0,2,1:T(4,128)S(1)} %multiply_add_fusion), kind=kOutput, calls=%fused_computation.3 | convolution fusion | flops 135266304 | bytes 17833984 | tf_op jit(solution)/shard_map/km,sm->ks/dot_general | solution.py:82
  76.4 18.1 %copy.34 = bf16[32,8,128,256]{3,1,2,0:T(8,128)(2,1)} copy(bf16[32,8,128,256]{3,2,1,0:T(8,128)(2,1)} %bitcast.34) | data formatting | bytes 33554432
  95.6 46.9 %all-gather.3.cloned.1.call-done = f32[32768,8]{0,1:T(8,128)} async-done(((f32[256,8]{0,1:T(8,128)}), f32[32768,8]{0,1:T(8,128)}) %all-gather.3.cloned.1.call-update) | async-done | bytes 1048592 | tf_op jit(solution)/shard_map/all_gather | solution.py:83
  142.5 1.4 reduce_sum.9
  143.8 8.1 %convolution_subtract_fusion = f32[8,32768]{1,0:T(8,128)S(1)} fusion(f32[8,32768]{1,0:T(8,128)S(1)} %bitcast.37, bf16[256,32768]{1,0:T(8,128)(2,1)} %bitcast.35, f32[256,8]{0,1:T(8,128)S(1)} %reduce_sum.9), kind=kOutput, calls=%fused_computation | convolution fusion | flops 134481920 | bytes 18882560 | tf_op jit(solution)/shard_map/ks,km->sm/dot_general | solution.py:86
  151.9 2.3 %fusion.59 = f32[8,8]{0,1:T(8,128)S(1)} fusion(f32[8,32768]{1,0:T(8,128)S(1)} %convolution_subtract_fusion), kind=kOutput, calls=%fused_computation.104 | convolution fusion | flops 25165824 | bytes 1048832 | tf_op jit(solution)/shard_map/dot_general | solution.py:89
  154.2 62.4 %psum.7 = f32[8,8]{0,1:T(8,128)S(1)} all-reduce(f32[8,8]{0,1:T(8,128)S(1)} %fusion.59), channel_id=1, replica_groups=mesh['role'=2,'slab'=64] {'role','slab'}, use_global_device_ids=true, to_apply=%region_1.0 | all-reduce | flops 64 | bytes 512 | tf_op jit(solution)/shard_map/psum | solution.py:90
  219.4 1.0 fusion.50
  220.4 1.3 copy.30
  (36 shorter events, 9.1 us)
Async XLA Ops:
  7.2 47.0 %copy-start = (f32[4,2,64,256]{3,2,1,0:T(8,128)S(1)}, f32[4,2,64,256]{3,2,1,0:T(8,128)}, u32[]{:S(2)}) copy-start(f32[4,2,64,256]{3,2,1,0:T(8,128)} %param.4) | copy-start | bytes 1572868
  7.2 135.3 %all-gather.3.cloned.1.call-start = ((), (), s32[]{:S(2)}) async-start(), calls=%async_computation | async-start | bytes 1056768 | tf_op jit(solution)/shard_map/all_gather | solution.py:83
  8.7 20.9 %collective-permute-start.1 = (f32[4,2,64,256]{3,0,2,1:T(4,128)S(1)}, f32[4,2,64,256]{3,0,2,1:T(4,128)S(1)}, u32[]{:S(2)}, u32[]{:S(2)}) collective-permute-start(f32[4,2,64,256]{3,0,2,1:T(4,128)S(1)} %copy.23), channel_id=1, source_target_pairs={{0,1},{1,2},{2,3},{3,4},{4,5},{5,6},{6,7},{7,8},{8,9},{9,10},{10,1... | collective-permute-start | bytes 1572872 | tf_op jit(solution)/shard_map/ppermute | solution.py:18
  11.2 18.4 %collective-permute-start = (f32[4,2,64,256]{3,0,2,1:T(4,128)S(1)}, f32[4,2,64,256]{3,0,2,1:T(4,128)S(1)}, u32[]{:S(2)}, u32[]{:S(2)}) collective-permute-start(f32[4,2,64,256]{3,0,2,1:T(4,128)S(1)} %copy.23), channel_id=1, source_target_pairs={{1,0},{2,1},{3,2},{4,3},{5,4},{6,5},{7,6},{8,7},{9,8},{10,9},{11,1... | collective-permute-start | bytes 1572872 | tf_op jit(solution)/shard_map/ppermute | solution.py:20
  18.0 8.3 %collective-permute-start.2 = (f32[4,2,2,256]{3,0,2,1:T(4,128)S(1)}, f32[4,2,2,256]{3,0,2,1:T(4,128)S(1)}, u32[]{:S(2)}, u32[]{:S(2)}) collective-permute-start(f32[4,2,2,256]{3,0,2,1:T(4,128)S(1)} %get-tuple-element.12), channel_id=1, source_target_pairs={{64,0},{65,1},{66,2},{67,3},{68,4},{69,5},{70,6},{71,7},{72,8},{73... | collective-permute-start | bytes 49160 | tf_op jit(solution)/shard_map/ppermute | solution.py:20
  20.9 4.0 %collective-permute-start.3 = (f32[4,2,2,256]{3,0,2,1:T(4,128)S(1)}, f32[4,2,2,256]{3,0,2,1:T(4,128)S(1)}, u32[]{:S(2)}, u32[]{:S(2)}) collective-permute-start(f32[4,2,2,256]{3,0,2,1:T(4,128)S(1)} %get-tuple-element.13), channel_id=1, source_target_pairs={{0,64},{1,65},{2,66},{3,67},{4,68},{5,69},{6,70},{7,71},{8,72},{9,... | collective-permute-start | bytes 49160 | tf_op jit(solution)/shard_map/ppermute | solution.py:18
  33.5 17.7 %collective-permute-start.5 = (f32[4,2,64,256]{3,0,2,1:T(4,128)S(1)}, f32[4,2,64,256]{3,0,2,1:T(4,128)S(1)}, u32[]{:S(2)}, u32[]{:S(2)}) collective-permute-start(f32[4,2,64,256]{3,0,2,1:T(4,128)S(1)} %multiply_add_fusion), channel_id=1, source_target_pairs={{0,1},{1,2},{2,3},{3,4},{4,5},{5,6},{6,7},{7,8},{8,9},{9,10},{10,1... | collective-permute-start | bytes 1572872 | tf_op jit(solution)/shard_map/ppermute | solution.py:18
  33.6 17.6 %collective-permute-start.4 = (f32[4,2,64,256]{3,0,2,1:T(4,128)S(1)}, f32[4,2,64,256]{3,0,2,1:T(4,128)S(1)}, u32[]{:S(2)}, u32[]{:S(2)}) collective-permute-start(f32[4,2,64,256]{3,0,2,1:T(4,128)S(1)} %multiply_add_fusion), channel_id=1, source_target_pairs={{1,0},{2,1},{3,2},{4,3},{5,4},{6,5},{7,6},{8,7},{9,8},{10,9},{11,1... | collective-permute-start | bytes 1572872 | tf_op jit(solution)/shard_map/ppermute | solution.py:20
  40.5 5.4 %collective-permute-start.6 = (f32[4,2,2,256]{3,0,2,1:T(4,128)S(1)}, f32[4,2,2,256]{3,0,2,1:T(4,128)S(1)}, u32[]{:S(2)}, u32[]{:S(2)}) collective-permute-start(f32[4,2,2,256]{3,0,2,1:T(4,128)S(1)} %get-tuple-element.10), channel_id=1, source_target_pairs={{64,0},{65,1},{66,2},{67,3},{68,4},{69,5},{70,6},{71,7},{72,8},{73... | collective-permute-start | bytes 49160 | tf_op jit(solution)/shard_map/ppermute | solution.py:20
  44.2 3.1 %collective-permute-start.7 = (f32[4,2,2,256]{3,0,2,1:T(4,128)S(1)}, f32[4,2,2,256]{3,0,2,1:T(4,128)S(1)}, u32[]{:S(2)}, u32[]{:S(2)}) collective-permute-start(f32[4,2,2,256]{3,0,2,1:T(4,128)S(1)} %get-tuple-element.11), channel_id=1, source_target_pairs={{0,64},{1,65},{2,66},{3,67},{4,68},{5,69},{6,70},{7,71},{8,72},{9,... | collective-permute-start | bytes 49160 | tf_op jit(solution)/shard_map/ppermute | solution.py:18
  143.8 78.6 %copy-start.1 = (f32[256,8]{0,1:T(8,128)}, f32[256,8]{0,1:T(8,128)S(1)}, u32[]{:S(2)}) copy-start(f32[256,8]{0,1:T(8,128)S(1)} %reduce_sum.9) | copy-start | bytes 24580
Sparse Core Ops, SparseCore 0:
  76.5 65.8 all-gather.2
